TPU v7x, 32 devices: a whole 2x2x4 slice. The times are simulated.
32 devices in a mesh: energy: 4 (over z), atom: 8 (over y, x, core).
Axes of the slice: x: 2, y: 2, z: 4, core: 2. Of those that a mesh axis runs over, the one named last changes fastest.
Arguments:
- t_mats: bfloat16 [4, 16, 2048], P('energy', 'atom'), may hold values from -0.75 to 0.75
- struct_table: bfloat16 [4, 64, 2048], P('energy'), may hold values from -0.359375 to 0.359375
- zone_atoms: int32 [16, 64], P('atom'), may hold values from 0 to 15, as said below
- zone_size: int32 [16], P('atom'), may hold values from 32 to 64
- pair_index: int32 [16, 384], P('atom'), may hold values from 0 to 63
- zone_link: int32 [16, 384], P('atom'), may hold values from 0 to 63
- weights: float32 [4, 2], P('energy'), may hold values from -1 to 1
Outputs:
- green: float32 [16, 2048], P('atom')
Inputs may be any that keep to these rules, and one draw needn't show every extreme that they name: Atom g is owned by index g // 2 of the atom axis; zone_atoms[g, 0] is g; the owner of every member of atom g's zone lies -4 to 3 steps from g's owner along the atom axis, counted around the axis, and both extreme offsets occur in every zone; members may repeat (periodic images).
All inputs are finite; a program needn't handle non-finite values.
Results may differ from a plain program's by a relative error of at most 0.003.
Values may be sent and summed in bfloat16 or wider, within the bound.
No kernel may reach another device: no remote copies, remote signals or barrier semaphores. Data moves between devices by JAX's collectives and lax.ppermute only.
A program may use at most 128 MiB of HBM per device.

v0:
```python
import jax
import jax.numpy as jnp
from jax import lax
from jax.sharding import PartitionSpec as P

L = 32
Z = 64
NB = 6


def real_form(block):
    parts = block.reshape(block.shape[:-1] + (2, L, L))
    real_part = parts[..., 0, :, :]
    imag_part = parts[..., 1, :, :]
    top_rows = jnp.concatenate([real_part, -imag_part], axis=-1)
    bottom_rows = jnp.concatenate([imag_part, real_part], axis=-1)
    return jnp.concatenate([top_rows, bottom_rows], axis=-2)


def take_rows(table, index):
    a_dev = index.shape[0]
    return jnp.take_along_axis(table, index.reshape(a_dev, -1), axis=1).reshape(index.shape)


def body(t_mats, struct_table, zone_atoms, zone_size, pair_index, zone_link, weights):
    e_dev, a_dev, block_flat = t_mats.shape
    window = lax.all_gather(t_mats, "atom", axis=1, tiled=True)
    coupling = jnp.arange(NB, dtype=jnp.int32)
    s2 = zone_link[:, :NB]
    s1 = take_rows(zone_link, s2[:, :, None] * NB + coupling)
    n1 = NB * NB
    slots = jnp.concatenate([s1.reshape(a_dev, n1), s2, jnp.zeros((a_dev, 1), jnp.int32)], axis=1)
    spots = slots[:, :, None] * NB + coupling
    pairs = take_rows(pair_index, spots)
    links = take_rows(zone_link, spots)
    members = take_rows(zone_atoms, slots)
    present = slots < zone_size[:, None]
    t_block = jnp.where(present[None, :, :, None], window[:, members], jnp.zeros((), jnp.bfloat16))
    t_real = real_form(t_block)
    g_real = real_form(struct_table[:, pairs])
    start_b = real_form(t_mats)[..., :L]
    start_f = start_b.astype(jnp.float32)
    is_zero = (slots == 0)[None, :, :, None, None]
    p1 = jnp.einsum(
        "easkij,eajc->easkic", g_real[:, :, :n1], start_b, preferred_element_type=jnp.float32
    )
    hit = (links[:, :n1] == 0)[None, :, :, :, None, None]
    coupled1 = jnp.sum(jnp.where(hit, p1, 0.0), axis=3).astype(jnp.bfloat16)
    col1 = jnp.einsum(
        "easij,easjc->easic", t_real[:, :, :n1], coupled1, preferred_element_type=jnp.float32
    ) + jnp.where(is_zero[:, :, :n1], start_f[:, :, None], 0.0)
    near2 = col1.astype(jnp.bfloat16).reshape(e_dev, a_dev, NB, NB, 2 * L, L)
    g2 = g_real[:, :, n1 : n1 + NB]
    coupled2 = jnp.einsum(
        "eamnij,eamnjc->eamic", g2, near2, preferred_element_type=jnp.float32
    ).astype(jnp.bfloat16)
    col2 = jnp.einsum(
        "eamij,eamjc->eamic",
        t_real[:, :, n1 : n1 + NB],
        coupled2,
        preferred_element_type=jnp.float32,
    ) + jnp.where(is_zero[:, :, n1 : n1 + NB], start_f[:, :, None], 0.0)
    near3 = col2.astype(jnp.bfloat16)
    coupled3 = jnp.einsum(
        "eanij,eanjc->eaic", g_real[:, :, n1 + NB], near3, preferred_element_type=jnp.float32
    ).astype(jnp.bfloat16)
    diagonal = (
        jnp.einsum(
            "eaij,eajc->eaic", t_real[:, :, n1 + NB], coupled3, preferred_element_type=jnp.float32
        )
        + start_f
    )
    real_rows = diagonal[:, :, :L, :].reshape(e_dev, a_dev, L * L)
    imag_rows = diagonal[:, :, L:, :].reshape(e_dev, a_dev, L * L)
    w_real = weights[:, 0][:, None, None]
    w_imag = weights[:, 1][:, None, None]
    green_real = jnp.sum(w_real * real_rows - w_imag * imag_rows, axis=0)
    green_imag = jnp.sum(w_real * imag_rows + w_imag * real_rows, axis=0)
    local_green = jnp.concatenate([green_real, green_imag], axis=-1)
    return lax.psum(local_green, "energy")


def solution(mesh):
    return jax.shard_map(
        body,
        mesh=mesh,
        in_specs=(
            P("energy", "atom", None),
            P("energy", None, None),
            P("atom", None),
            P("atom"),
            P("atom", None),
            P("atom", None),
            P("energy", None),
        ),
        out_specs=P("atom", None),
        check_vma=False,
    )
```

profile of v0, /device:TPU:0, one launch (start us, length us, event | category | flops | bytes accessed | tf_op | source)
XLA Modules:
  0.0 100.4 jit_solution(1606972806575443180)
XLA Ops:
  0.0 0.8 slice_bitcast_fusion.6
  1.1 2.2 %gather_fusion.2 = s32[72]{0:T(128)S(1)} fusion(s32[2,384]{1,0:T(2,128)} %param.14, s32[72]{0:T(128)S(1)} %reshape.652), kind=kCustom, calls=%fused_computation.4 | custom fusion | bytes 1152 | tf_op jit(solution)/shard_map/jit(take_along_axis)/gather | solution.py:22
  3.7 0.1 add.215
  3.9 0.1 add.217
  4.1 9.7 %gather_fusion.4 = s32[516]{0:T(1024)S(1)} fusion(s32[2,384]{1,0:T(2,128)} %param.13, s32[516]{0:T(1024)S(1)} %reshape.682), kind=kCustom, calls=%fused_computation.clone | custom fusion | bytes 8256 | tf_op jit(solution)/shard_map/jit(take_along_axis)/gather | solution.py:22
  13.9 7.5 %gather_fusion.5 = s32[516]{0:T(1024)S(1)} fusion(s32[2,384]{1,0:T(2,128)S(1)} %copy-done.1, s32[516]{0:T(1024)S(1)} %reshape.682), kind=kCustom, calls=%fused_computation.1.clone | custom fusion | bytes 8256 | tf_op jit(solution)/shard_map/jit(take_along_axis)/gather | solution.py:22
  21.6 0.1 reshape.614
  21.7 0.1 reshape.608
  21.8 0.1 reshape.646
  22.0 3.4 %gather_fusion.1 = bf16[516,2048]{1,0:T(8,128)(2,1)S(1)} fusion(bf16[64,2048]{1,0:T(8,128)(2,1)S(1)} %bitcast.108, s32[1024]{0:T(1024)S(1)} %pad_clamp_fusion), kind=kCustom, calls=%fused_computation.3 | custom fusion | bytes 4229136 | tf_op jit(solution)/shard_map/gather | solution.py:40
  25.4 9.3 %reshape.609 = bf16[1,2,43,6,2,32,32]{6,5,4,3,2,1,0:T(8,128)(2,1)} reshape(bf16[516,2048]{1,0:T(8,128)(2,1)S(1)} %gather_fusion.1) | data formatting | bytes 4227072 | tf_op jit(solution)/shard_map/reshape | solution.py:12
  34.7 7.3 %slice_bitcast_fusion = (bf16[1,2,43,6,32,32]{5,4,3,2,1,0:T(8,128)(2,1)}, bf16[1,2,43,6,32,32]{5,4,3,2,1,0:T(8,128)(2,1)}) fusion(bf16[1,2,43,6,2,32,32]{6,5,4,3,2,1,0:T(8,128)(2,1)} %reshape.609), kind=kLoop, calls=%fused_computation.14 | loop fusion | bytes 4227072 | tf_op jit(solution)/shard_map/squeeze | solution.py:14
  42.1 1.5 %copy-done.3 = bf16[1,2,43,6,2,32,32]{6,5,4,3,2,1,0:T(8,128)(2,1)S(1)} copy-done((bf16[1,2,43,6,2,32,32]{6,5,4,3,2,1,0:T(8,128)(2,1)S(1)}, bf16[1,2,43,6,2,32,32]{6,5,4,3,2,1,0:T(8,128)(2,1)}, u32[]{:S(2)}) %copy-start.3) | copy-done | bytes 2113560
  43.6 2.5 %fusion.70 = bf16[1,2,43,6,32,32]{5,4,3,2,1,0:T(8,128)(2,1)} fusion(bf16[1,2,43,6,2,32,32]{6,5,4,3,2,1,0:T(8,128)(2,1)S(1)} %copy-done.3), kind=kLoop, calls=%fused_computation.115 | loop fusion | flops 528384 | bytes 2113536 | tf_op jit(solution)/shard_map/neg | solution.py:15
  46.5 9.5 %select_reduce_fusion = bf16[2,36,64,32]{2,3,1,0:T(8,128)(2,1)S(1)} fusion(pred[2,36,6]{2,1,0:T(8,128)(4,1)S(1)} %slice_compare_fusion, bf16[1,2,43,6,32,32]{5,4,3,2,1,0:T(8,128)(2,1)} %get-tuple-element.13, bf16[1,2,43,6,32,32]{5,4,3,2,1,0:T(8,128)(2,1)} %get-tuple-element.12, bf16[1,2,43,6,32,32]{5,4,3,2,1,0:T(8,128)(2,1)} %fusion.70, ...), kind=kOutput, calls=%fused_computation.13 | convolution fusion | flops 129024000 | bytes 3473840 | tf_op jit(solution)/shard_map/easkij,eajc->easkic/dot_general | solution.py:44
  56.2 2.0 %gather_fusion.3 = s32[86]{0:T(128)S(1)} fusion(s32[2,64]{1,0:T(2,128)S(1)} %copy-done.2, s32[86]{0:T(128)S(1)} %reshape.658), kind=kCustom, calls=%fused_computation.5 | custom fusion | bytes 1376 | tf_op jit(solution)/shard_map/jit(take_along_axis)/gather | solution.py:22
  58.4 10.7 %all_gather.3 = bf16[1,16,2048]{2,0,1:T(2,128)(2,1)S(1)} all-gather(bf16[1,2,2048]{2,0,1:T(2,128)(2,1)S(1)} %copy.27), channel_id=1, replica_groups=mesh['energy'=4,'atom'=8] {'atom'}, dimensions={1}, use_global_device_ids=true | all-gather | bytes 73728 | tf_op jit(solution)/shard_map/all_gather | solution.py:27
  69.1 0.8 gather_fusion
  69.9 1.1 %reshape.694 = bf16[1,2,43,2,32,32]{5,4,3,2,1,0:T(8,128)(2,1)S(1)} reshape(bf16[86,2048]{1,0:T(8,128)(2,1)S(1)} %gather_fusion) | data formatting | bytes 704512 | tf_op jit(solution)/shard_map/gather | solution.py:38
  71.1 0.2 copy_select_fusion
  71.3 0.3 slice_bitcast_fusion.2
  71.6 0.1 fusion.69
  71.8 0.9 fusion.8
  72.8 0.6 copy-done.5
  73.3 1.3 %slice-done.1 = s8[4194304]{0:T(1024)(128)(4,1)S(1)} async-done(((s8[4227072]{0:T(1024)(128)(4,1)}), s8[4194304]{0:T(1024)(128)(4,1)S(1)}, s32[]{:S(2)}) %slice-start.1) | async-done | bytes 4194328
  74.7 1.3 %copy-done.4 = bf16[1,2,43,6,32,32]{5,4,3,2,1,0:T(8,128)(2,1)S(1)} copy-done((bf16[1,2,43,6,32,32]{5,4,3,2,1,0:T(8,128)(2,1)S(1)}, bf16[1,2,43,6,32,32]{5,4,3,2,1,0:T(8,128)(2,1)}, u32[]{:S(2)}) %copy-start.4) | copy-done | bytes 1056792
  75.9 0.8 fusion.23
  76.8 1.5 %fusion.27 = bf16[2,64,32]{1,2,0:T(8,128)(2,1)S(1)} fusion(bf16[2,6,64,32]{2,3,1,0:T(8,128)(2,1)S(1)} %fusion.23, bf16[1,2,43,32,32]{4,3,2,1,0:T(8,128)(2,1)S(1)} %get-tuple-element.15, bf16[1,2,43,32,32]{4,3,2,1,0:T(8,128)(2,1)S(1)} %get-tuple-element.14, bf16[1,2,43,32,32]{4,3,2,1,0:T(8,128)(2,1)S(1)} %fusion.69, ...), kind=kOutput, calls=%fused_computation.41 | convolution fusion | flops 7155712 | bytes 3772428 | tf_op jit(solution)/shard_map/eanij,eanjc->eaic/dot_general | solution.py:64
  78.2 0.2 fusion.26
  78.5 0.6 fusion.73
  79.1 1.4 %multiply_subtract_fusion = (f32[1,2,32,32]{2,3,1,0:T(8,128)S(1)}, f32[1,2,32,32]{2,3,1,0:T(8,128)S(1)}) fusion(f32[1,2,64,32]{2,3,1,0:T(8,128)S(1)} %fusion.26, f32[]{:T(128)} %bitcast.32, f32[]{:T(128)} %bitcast), kind=kLoop, calls=%fused_computation.75 | loop fusion | flops 12288 | bytes 32776 | tf_op jit(solution)/shard_map/sub | solution.py:77
  80.8 19.6 %psum.7 = f32[2,2048]{1,0:T(2,128)} all-reduce(f32[2,2048]{1,0:T(2,128)S(1)} %pad_maximum_fusion.8), channel_id=1, replica_groups=mesh['energy'=4,'atom'=8] {'energy'}, use_global_device_ids=true, to_apply=%region_1.0 | all-reduce | flops 4096 | bytes 32768 | tf_op jit(solution)/shard_map/psum | solution.py:80
  (64 shorter events, 2.4 us)
Async XLA Ops:
  0.0 22.0 %copy-start = (bf16[1,64,2048]{2,1,0:T(8,128)(2,1)S(1)}, bf16[1,64,2048]{2,1,0:T(8,128)(2,1)}, u32[]{:S(2)}) copy-start(bf16[1,64,2048]{2,1,0:T(8,128)(2,1)} %param.10) | copy-start | bytes 786436
  0.0 13.9 %copy-start.1 = (s32[2,384]{1,0:T(2,128)S(1)}, s32[2,384]{1,0:T(2,128)}, u32[]{:S(2)}) copy-start(s32[2,384]{1,0:T(2,128)} %param.14) | copy-start | bytes 9220
  34.7 8.9 %copy-start.3 = (bf16[1,2,43,6,2,32,32]{6,5,4,3,2,1,0:T(8,128)(2,1)S(1)}, bf16[1,2,43,6,2,32,32]{6,5,4,3,2,1,0:T(8,128)(2,1)}, u32[]{:S(2)}) copy-start(bf16[1,2,43,6,2,32,32]{6,5,4,3,2,1,0:T(8,128)(2,1)} %reshape.609) | copy-start | bytes 6340612
  43.6 2.5 %copy-start.6 = (bf16[1,2,2048]{2,1,0:T(2,128)(2,1)S(1)}, bf16[1,2,2048]{2,1,0:T(2,128)(2,1)}, u32[]{:S(2)}) copy-start(bf16[1,2,2048]{2,1,0:T(2,128)(2,1)} %param.9) | copy-start | bytes 24580
  46.5 9.7 %copy-start.2 = (s32[2,64]{1,0:T(2,128)S(1)}, s32[2,64]{1,0:T(2,128)}, u32[]{:S(2)}) copy-start(s32[2,64]{1,0:T(2,128)} %param.11) | copy-start | bytes 1540
  56.0 15.1 %copy-start.8 = (s32[2]{0:T(128)S(1)}, s32[2]{0:T(128)}, u32[]{:S(2)}) copy-start(s32[2]{0:T(128)} %param.12) | copy-start | bytes 28
  69.9 2.8 %slice-start = ((s8[4227072]{0:T(1024)(128)(4,1)}), s8[32768]{0:T(1024)(128)(4,1)S(1)}, s32[]{:S(2)}) async-start(s8[4227072]{0:T(1024)(128)(4,1)} %bitcast.110), calls=%async_computation | async-start | bytes 65536
  71.1 2.2 %copy-start.5 = (bf16[1,2,43,6,32,32]{5,4,3,2,1,0:T(8,128)(2,1)S(1)}, bf16[1,2,43,6,32,32]{5,4,3,2,1,0:T(8,128)(2,1)}, u32[]{:S(2)}) copy-start(bf16[1,2,43,6,32,32]{5,4,3,2,1,0:T(8,128)(2,1)} %get-tuple-element.13) | copy-start | bytes 3170308
  71.3 3.3 %slice-start.1 = ((s8[4227072]{0:T(1024)(128)(4,1)}), s8[4194304]{0:T(1024)(128)(4,1)S(1)}, s32[]{:S(2)}) async-start(s8[4227072]{0:T(1024)(128)(4,1)} %bitcast.110), calls=%async_computation.1 | async-start | bytes 8388608
  71.6 4.3 %copy-start.4 = (bf16[1,2,43,6,32,32]{5,4,3,2,1,0:T(8,128)(2,1)S(1)}, bf16[1,2,43,6,32,32]{5,4,3,2,1,0:T(8,128)(2,1)}, u32[]{:S(2)}) copy-start(bf16[1,2,43,6,32,32]{5,4,3,2,1,0:T(8,128)(2,1)} %get-tuple-element.12) | copy-start | bytes 3170308
  76.8 1.7 %copy-start.7 = (f32[1,2]{1,0:T(1,128)S(1)}, f32[1,2]{1,0:T(1,128)}, u32[]{:S(2)}) copy-start(f32[1,2]{1,0:T(1,128)} %param.15) | copy-start | bytes 28
where the time goes:
time: 101 us; the launch traced here: 100 us
  local copies, waits for them, and re-layouts  51.6 us (51%)
  blocking collectives  30.3 us (30%)
  matrix products  12.9 us (13%)
  other arithmetic  5.4 us (5%)
    gather x11, local copies, waits for them, and re-layouts, take_rows(): jnp.take_along_axis(table, index.reshape(a_dev, -1), axis=1)  22.1 us
    psum x1, blocking collectives, body(): return lax.psum(local_green, 'energy')  19.6 us
    all_gather x1, blocking collectives, body(): window = lax.all_gather(t_mats, 'atom', axis=1, tiled=True)  10.7 us
    dot_general x1, matrix products, body(): jnp.einsum('easkij,eajc->easkic', g_real[:, :, :n1], start_b, preferred_e...  9.49 us
    reshape x2, local copies, waits for them, and re-layouts, real_form(): parts = block.reshape(block.shape[:-1] + (2, L, L))  9.42 us
    squeeze x2, local copies, waits for them, and re-layouts, real_form(): imag_part = parts[..., 1, :, :]  7.6 us
    unnamed x26, local copies, waits for them, and re-layouts  4.99 us
    gather x1, local copies, waits for them, and re-layouts, body(): g_real = real_form(struct_table[:, pairs])  3.39 us

commit v1 on v0

--- a/solution.py
+++ b/solution.py
@@ -1,3 +1,4 @@
+import functools
 import jax
 import jax.numpy as jnp
 from jax import lax
@@ -6,6 +7,13 @@
 L = 32
 Z = 64
 NB = 6
+
+
+def _hold_map(page, axis_id):
+    return jax.lax.all_gather(page, axis_id).sum(axis=0)
+
+
+end_the_sector = functools.partial(_hold_map, axis_id="energy")
 
 
 def real_form(block):
@@ -77,7 +85,7 @@
     green_real = jnp.sum(w_real * real_rows - w_imag * imag_rows, axis=0)
     green_imag = jnp.sum(w_real * imag_rows + w_imag * real_rows, axis=0)
     local_green = jnp.concatenate([green_real, green_imag], axis=-1)
-    return lax.psum(local_green, "energy")
+    return end_the_sector(local_green)
 
 
 def solution(mesh):

time: 101 us -> 95 us (0.941)
  blocking collectives: 30.3 us -> 24 us
    psum x1 -> x0, blocking collectives: 19.6 us -> none  [body(): return lax.psum(local_green, 'energy')]
    all_gather x0 -> x1, blocking collectives: none -> 13.4 us  [_hold_map(): return jax.lax.all_gather(page, axis_id).sum(axis=0)]
where the time goes in v1:
time: 95 us; the launch traced here: 94.8 us
  local copies, waits for them, and re-layouts  51.6 us (54%)
  blocking collectives  24 us (25%)
  matrix products  12.9 us (14%)
  other arithmetic  6.04 us (6%)
    gather x11, local copies, waits for them, and re-layouts, take_rows(): jnp.take_along_axis(table, index.reshape(a_dev, -1), axis=1)  22.1 us
    all_gather x1, blocking collectives, _hold_map(): return jax.lax.all_gather(page, axis_id).sum(axis=0)  13.4 us
    all_gather x1, blocking collectives, body(): window = lax.all_gather(t_mats, 'atom', axis=1, tiled=True)  10.7 us
    dot_general x1, matrix products, body(): jnp.einsum('easkij,eajc->easkic', g_real[:, :, :n1], start_b, preferred_e...  9.49 us
    reshape x2, local copies, waits for them, and re-layouts, real_form(): parts = block.reshape(block.shape[:-1] + (2, L, L))  9.42 us
    squeeze x2, local copies, waits for them, and re-layouts, real_form(): imag_part = parts[..., 1, :, :]  7.6 us
    unnamed x26, local copies, waits for them, and re-layouts  4.99 us
    gather x1, local copies, waits for them, and re-layouts, body(): g_real = real_form(struct_table[:, pairs])  3.39 us

profile of v1, /device:TPU:0, one launch (start us, length us, event | category | flops | bytes accessed | tf_op | source)
XLA Modules:
  0.0 94.8 jit_solution(12903183545365849367)
XLA Ops:
  0.0 0.8 slice_bitcast_fusion.6
  1.1 2.2 %gather_fusion.2 = s32[72]{0:T(128)S(1)} fusion(s32[2,384]{1,0:T(2,128)} %param.14, s32[72]{0:T(128)S(1)} %reshape.652), kind=kCustom, calls=%fused_computation.4 | custom fusion | bytes 1152 | tf_op jit(solution)/shard_map/jit(take_along_axis)/gather | solution.py:30
  3.7 0.1 add.213
  3.9 0.1 add.215
  4.1 9.7 %gather_fusion.4 = s32[516]{0:T(1024)S(1)} fusion(s32[2,384]{1,0:T(2,128)} %param.13, s32[516]{0:T(1024)S(1)} %reshape.686), kind=kCustom, calls=%fused_computation.clone | custom fusion | bytes 8256 | tf_op jit(solution)/shard_map/jit(take_along_axis)/gather | solution.py:30
  13.9 7.5 %gather_fusion.5 = s32[516]{0:T(1024)S(1)} fusion(s32[2,384]{1,0:T(2,128)S(1)} %copy-done.1, s32[516]{0:T(1024)S(1)} %reshape.686), kind=kCustom, calls=%fused_computation.1.clone | custom fusion | bytes 8256 | tf_op jit(solution)/shard_map/jit(take_along_axis)/gather | solution.py:30
  21.6 0.1 reshape.614
  21.7 0.1 reshape.608
  21.8 0.1 reshape.646
  22.0 3.4 %gather_fusion.1 = bf16[516,2048]{1,0:T(8,128)(2,1)S(1)} fusion(bf16[64,2048]{1,0:T(8,128)(2,1)S(1)} %bitcast.110, s32[1024]{0:T(1024)S(1)} %pad_clamp_fusion), kind=kCustom, calls=%fused_computation.3 | custom fusion | bytes 4229136 | tf_op jit(solution)/shard_map/gather | solution.py:48
  25.4 9.3 %reshape.609 = bf16[1,2,43,6,2,32,32]{6,5,4,3,2,1,0:T(8,128)(2,1)} reshape(bf16[516,2048]{1,0:T(8,128)(2,1)S(1)} %gather_fusion.1) | data formatting | bytes 4227072 | tf_op jit(solution)/shard_map/reshape | solution.py:20
  34.7 7.3 %slice_bitcast_fusion = (bf16[1,2,43,6,32,32]{5,4,3,2,1,0:T(8,128)(2,1)}, bf16[1,2,43,6,32,32]{5,4,3,2,1,0:T(8,128)(2,1)}) fusion(bf16[1,2,43,6,2,32,32]{6,5,4,3,2,1,0:T(8,128)(2,1)} %reshape.609), kind=kLoop, calls=%fused_computation.14 | loop fusion | bytes 4227072 | tf_op jit(solution)/shard_map/squeeze | solution.py:22
  42.1 1.5 %copy-done.3 = bf16[1,2,43,6,2,32,32]{6,5,4,3,2,1,0:T(8,128)(2,1)S(1)} copy-done((bf16[1,2,43,6,2,32,32]{6,5,4,3,2,1,0:T(8,128)(2,1)S(1)}, bf16[1,2,43,6,2,32,32]{6,5,4,3,2,1,0:T(8,128)(2,1)}, u32[]{:S(2)}) %copy-start.3) | copy-done | bytes 2113560
  43.6 2.5 %fusion.70 = bf16[1,2,43,6,32,32]{5,4,3,2,1,0:T(8,128)(2,1)} fusion(bf16[1,2,43,6,2,32,32]{6,5,4,3,2,1,0:T(8,128)(2,1)S(1)} %copy-done.3), kind=kLoop, calls=%fused_computation.115 | loop fusion | flops 528384 | bytes 2113536 | tf_op jit(solution)/shard_map/neg | solution.py:23
  46.5 9.5 %select_reduce_fusion = bf16[2,36,64,32]{2,3,1,0:T(8,128)(2,1)S(1)} fusion(pred[2,36,6]{2,1,0:T(8,128)(4,1)S(1)} %slice_compare_fusion, bf16[1,2,43,6,32,32]{5,4,3,2,1,0:T(8,128)(2,1)} %get-tuple-element.13, bf16[1,2,43,6,32,32]{5,4,3,2,1,0:T(8,128)(2,1)} %get-tuple-element.12, bf16[1,2,43,6,32,32]{5,4,3,2,1,0:T(8,128)(2,1)} %fusion.70, ...), kind=kOutput, calls=%fused_computation.13 | convolution fusion | flops 129024000 | bytes 3473840 | tf_op jit(solution)/shard_map/easkij,eajc->easkic/dot_general | solution.py:52
  56.2 2.0 %gather_fusion.3 = s32[86]{0:T(128)S(1)} fusion(s32[2,64]{1,0:T(2,128)S(1)} %copy-done.2, s32[86]{0:T(128)S(1)} %reshape.658), kind=kCustom, calls=%fused_computation.5 | custom fusion | bytes 1376 | tf_op jit(solution)/shard_map/jit(take_along_axis)/gather | solution.py:30
  58.4 10.7 %all_gather.9 = bf16[1,16,2048]{2,0,1:T(2,128)(2,1)S(1)} all-gather(bf16[1,2,2048]{2,0,1:T(2,128)(2,1)S(1)} %copy.27), channel_id=1, replica_groups=mesh['energy'=4,'atom'=8] {'atom'}, dimensions={1}, use_global_device_ids=true | all-gather | bytes 73728 | tf_op jit(solution)/shard_map/all_gather | solution.py:35
  69.1 0.8 gather_fusion
  69.9 1.1 %reshape.698 = bf16[1,2,43,2,32,32]{5,4,3,2,1,0:T(8,128)(2,1)S(1)} reshape(bf16[86,2048]{1,0:T(8,128)(2,1)S(1)} %gather_fusion) | data formatting | bytes 704512 | tf_op jit(solution)/shard_map/gather | solution.py:46
  71.1 0.2 copy_select_fusion
  71.3 0.3 slice_bitcast_fusion.2
  71.8 0.9 %fusion.8 = bf16[2,36,64,32]{2,3,1,0:T(8,128)(2,1)S(1)} fusion(bf16[1,2,43,32,32]{4,3,2,1,0:T(8,128)(2,1)S(1)} %get-tuple-element.15, bf16[1,2,43,32,32]{4,3,2,1,0:T(8,128)(2,1)S(1)} %get-tuple-element.14, bf16[1,2,43,32,32]{4,3,2,1,0:T(8,128)(2,1)S(1)} %fusion.69, f32[2,64,32]{1,2,0:T(8,128)S(1)} %get-tuple-element.8, ...), kind=kOutput, calls=%fused_computation.18 | convolution fusion | flops 21676032 | bytes 1134664 | tf_op jit(solution)/shard_map/easij,easjc->easic/dot_general | solution.py:57
  72.8 0.6 copy-done.5
  73.3 1.3 %slice-done.1 = s8[4194304]{0:T(1024)(128)(4,1)S(1)} async-done(((s8[4227072]{0:T(1024)(128)(4,1)}), s8[4194304]{0:T(1024)(128)(4,1)S(1)}, s32[]{:S(2)}) %slice-start.1) | async-done | bytes 4194328
  74.7 1.3 %copy-done.4 = bf16[1,2,43,6,32,32]{5,4,3,2,1,0:T(8,128)(2,1)S(1)} copy-done((bf16[1,2,43,6,32,32]{5,4,3,2,1,0:T(8,128)(2,1)S(1)}, bf16[1,2,43,6,32,32]{5,4,3,2,1,0:T(8,128)(2,1)}, u32[]{:S(2)}) %copy-start.4) | copy-done | bytes 1056792
  75.9 0.8 fusion.23
  76.8 1.5 %fusion.27 = bf16[2,64,32]{1,2,0:T(8,128)(2,1)S(1)} fusion(bf16[2,6,64,32]{2,3,1,0:T(8,128)(2,1)S(1)} %fusion.23, bf16[1,2,43,32,32]{4,3,2,1,0:T(8,128)(2,1)S(1)} %get-tuple-element.15, bf16[1,2,43,32,32]{4,3,2,1,0:T(8,128)(2,1)S(1)} %get-tuple-element.14, bf16[1,2,43,32,32]{4,3,2,1,0:T(8,128)(2,1)S(1)} %fusion.69, ...), kind=kOutput, calls=%fused_computation.41 | convolution fusion | flops 7155712 | bytes 3772428 | tf_op jit(solution)/shard_map/eanij,eanjc->eaic/dot_general | solution.py:72
  78.2 0.2 fusion.26
  78.5 0.6 fusion.73
  79.1 1.4 %multiply_subtract_fusion = (f32[1,2,32,32]{2,3,1,0:T(8,128)S(1)}, f32[1,2,32,32]{2,3,1,0:T(8,128)S(1)}) fusion(f32[1,2,64,32]{2,3,1,0:T(8,128)S(1)} %fusion.26, f32[]{:T(128)} %bitcast.32, f32[]{:T(128)} %bitcast), kind=kLoop, calls=%fused_computation.75 | loop fusion | flops 12288 | bytes 32776 | tf_op jit(solution)/shard_map/sub | solution.py:85
  80.8 13.4 %all-gather.1 = f32[4,2,2048]{2,1,0:T(2,128)S(1)} all-gather(f32[1,2,2048]{2,1,0:T(2,128)S(1)} %maximum_bitcast_fusion.13), channel_id=2, replica_groups=mesh['energy'=4,'atom'=8] {'energy'}, dimensions={0}, use_global_device_ids=true | all-gather | bytes 81920 | tf_op jit(solution)/shard_map/all_gather | solution.py:13
  94.1 0.6 reduce_sum.20
  (65 shorter events, 2.5 us)
Async XLA Ops:
  0.0 22.0 %copy-start = (bf16[1,64,2048]{2,1,0:T(8,128)(2,1)S(1)}, bf16[1,64,2048]{2,1,0:T(8,128)(2,1)}, u32[]{:S(2)}) copy-start(bf16[1,64,2048]{2,1,0:T(8,128)(2,1)} %param.10) | copy-start | bytes 786436
  0.0 13.9 %copy-start.1 = (s32[2,384]{1,0:T(2,128)S(1)}, s32[2,384]{1,0:T(2,128)}, u32[]{:S(2)}) copy-start(s32[2,384]{1,0:T(2,128)} %param.14) | copy-start | bytes 9220
  34.7 8.9 %copy-start.3 = (bf16[1,2,43,6,2,32,32]{6,5,4,3,2,1,0:T(8,128)(2,1)S(1)}, bf16[1,2,43,6,2,32,32]{6,5,4,3,2,1,0:T(8,128)(2,1)}, u32[]{:S(2)}) copy-start(bf16[1,2,43,6,2,32,32]{6,5,4,3,2,1,0:T(8,128)(2,1)} %reshape.609) | copy-start | bytes 6340612
  43.6 2.5 %copy-start.6 = (bf16[1,2,2048]{2,1,0:T(2,128)(2,1)S(1)}, bf16[1,2,2048]{2,1,0:T(2,128)(2,1)}, u32[]{:S(2)}) copy-start(bf16[1,2,2048]{2,1,0:T(2,128)(2,1)} %param.9) | copy-start | bytes 24580
  46.5 9.7 %copy-start.2 = (s32[2,64]{1,0:T(2,128)S(1)}, s32[2,64]{1,0:T(2,128)}, u32[]{:S(2)}) copy-start(s32[2,64]{1,0:T(2,128)} %param.11) | copy-start | bytes 1540
  56.0 15.1 %copy-start.8 = (s32[2]{0:T(128)S(1)}, s32[2]{0:T(128)}, u32[]{:S(2)}) copy-start(s32[2]{0:T(128)} %param.12) | copy-start | bytes 28
  69.9 2.8 %slice-start = ((s8[4227072]{0:T(1024)(128)(4,1)}), s8[32768]{0:T(1024)(128)(4,1)S(1)}, s32[]{:S(2)}) async-start(s8[4227072]{0:T(1024)(128)(4,1)} %bitcast.112), calls=%async_computation | async-start | bytes 65536
  71.1 2.2 %copy-start.5 = (bf16[1,2,43,6,32,32]{5,4,3,2,1,0:T(8,128)(2,1)S(1)}, bf16[1,2,43,6,32,32]{5,4,3,2,1,0:T(8,128)(2,1)}, u32[]{:S(2)}) copy-start(bf16[1,2,43,6,32,32]{5,4,3,2,1,0:T(8,128)(2,1)} %get-tuple-element.13) | copy-start | bytes 3170308
  71.3 3.3 %slice-start.1 = ((s8[4227072]{0:T(1024)(128)(4,1)}), s8[4194304]{0:T(1024)(128)(4,1)S(1)}, s32[]{:S(2)}) async-start(s8[4227072]{0:T(1024)(128)(4,1)} %bitcast.112), calls=%async_computation.1 | async-start | bytes 8388608
  71.6 4.3 %copy-start.4 = (bf16[1,2,43,6,32,32]{5,4,3,2,1,0:T(8,128)(2,1)S(1)}, bf16[1,2,43,6,32,32]{5,4,3,2,1,0:T(8,128)(2,1)}, u32[]{:S(2)}) copy-start(bf16[1,2,43,6,32,32]{5,4,3,2,1,0:T(8,128)(2,1)} %get-tuple-element.12) | copy-start | bytes 3170308
  76.8 1.7 %copy-start.7 = (f32[1,2]{1,0:T(1,128)S(1)}, f32[1,2]{1,0:T(1,128)}, u32[]{:S(2)}) copy-start(f32[1,2]{1,0:T(1,128)} %param.15) | copy-start | bytes 28
